TPU v7x, 256 devices: a whole 4x4x8 slice. The times are simulated.
256 devices in a mesh: bus: 16 (over y, z_hi), line: 16 (over z_lo, x, core).
Axes of the slice: x: 4, y: 4, z: 8 (z_hi: 4, z_lo: 2; z = z_hi * 2 + z_lo), core: 2. Of those that a mesh axis runs over, the one named last changes fastest.
Arguments:
- generation: bfloat16 [1024, 16384], P(None, 'bus'), may hold values from -6 to 6
- profiles: float32 [24, 16384], P(None, 'bus'), may hold values from -5 to 5
- scen_profile: int32 [1024], replicated, may hold values from 0 to 23
- ptdf: bfloat16 [16384, 16384], P('line', 'bus'), may hold values from -0.046875 to 0.046875
- lodf: float32 [6144, 512], P('line'), may hold values from -1 to 1
- limits: float32 [6144], P('line'), may hold values from 0.5 to 2
- monitored: int32 [6144], P('line'), may hold values from 0 to 16383, as said below
- outages: int32 [512], replicated, may hold values from 0 to 16383, as said below
- cost_quad: float32 [16384], P('bus'), may hold values from 0.5 to 2
Outputs:
- gradient: bfloat16 [1024, 16384], P('line', 'bus')
- outage_flow: float32 [1024, 512], P('bus')
- outage_sens: float32 [1024, 512], P('bus')
Inputs may be any that keep to these rules, and one draw needn't show every extreme that they name: `monitored`: the entries with positions k * 384 to (k + 1) * 384 - 1 are distinct line ids of the k-th block of 1024 lines (ids k * 1024 to (k + 1) * 1024 - 1). `outages`: distinct line ids; how many fall in each block of 1024 lines varies from block to block.
All inputs are finite; a program needn't handle non-finite values.
Results may differ from a plain program's by a relative error of at most 0.0029.
Values may be sent and summed in bfloat16 or wider, within the bound.
No kernel may reach another device: no remote copies, remote signals or barrier semaphores. Data moves between devices by JAX's collectives and lax.ppermute only.
A program may use at most 64 MiB of HBM per device.

v0:
```python
import math
import jax
import jax.numpy as jnp
from jax import lax
from jax.sharding import PartitionSpec as P

sharpness = 4.0


def contingency(pieces, lodf, limits, outage_total):
    base_block, outage_block = pieces
    post_flow = base_block[:, :, None] + lodf[None, :, :] * outage_block[:, None, :]
    bounds = limits[None, :, None]
    raw_slope = jax.nn.sigmoid(sharpness * (post_flow - bounds)) - jax.nn.sigmoid(
        sharpness * (-post_flow - bounds)
    )
    direct = jnp.sum(raw_slope, axis=2) / outage_total
    sens_part = jnp.einsum("smk,mk->sk", raw_slope, lodf, precision=lax.Precision.HIGHEST)
    return (direct, sens_part)


def on_device(
    generation, profiles, scen_profile, ptdf, lodf, limits, monitored, outages, cost_quad
):
    profile_count = profiles.shape[0]
    profile_pick = (
        scen_profile[:, None] == jnp.arange(profile_count, dtype=jnp.int32)[None, :]
    ).astype(jnp.float32)
    loads = jnp.dot(profile_pick, profiles, precision=lax.Precision.HIGHEST)
    injection = (generation.astype(jnp.float32) - loads).astype(jnp.bfloat16)
    scen_rows = injection.shape[0] // lax.axis_size("bus")
    line_rows = ptdf.shape[0]
    first_line = lax.axis_index("line") * line_rows
    local_monitored = monitored - first_line
    positions = jnp.arange(line_rows, dtype=jnp.int32)
    picker = ((outages - first_line)[None, :] == positions[:, None]).astype(jnp.float32)
    monitor_count = monitored.shape[0]
    inputs = injection
    flow_field = lax.psum_scatter(
        lax.dot_general(inputs, ptdf, (((1,), (1,)), ((), ())), preferred_element_type=jnp.float32),
        "bus",
        scatter_dimension=0,
        tiled=True,
    )
    base = jnp.take(flow_field, local_monitored, axis=1)
    entire_flows = lax.all_gather(flow_field, "line", axis=1, tiled=True)
    outflow = jnp.take(entire_flows, outages, axis=1)
    outage_total = outages.shape[0]
    monitored_total = monitor_count * lax.axis_size("line")
    block_size = math.gcd(scen_rows, 4)
    base_blocks = base.reshape(scen_rows // block_size, block_size, monitor_count)
    outage_blocks = outflow.reshape(scen_rows // block_size, block_size, outage_total)
    direct, sens_part = lax.map(
        lambda pieces: contingency(pieces, lodf, limits, outage_total), (base_blocks, outage_blocks)
    )
    direct = direct.reshape(scen_rows, monitor_count)
    sens_part = sens_part.reshape(scen_rows, outage_total)
    sens_total = lax.psum(sens_part, "line")
    backward = sens_total / outage_total
    outage_sens = sens_total / math.sqrt(monitored_total)
    adjoint = jnp.zeros((scen_rows, line_rows), jnp.float32).at[:, local_monitored].add(direct)
    adjoint = adjoint + jnp.dot(backward, picker.T, precision=lax.Precision.HIGHEST)
    adjoint_half = adjoint.astype(jnp.bfloat16)
    all_adjoint = lax.all_gather(adjoint_half, "bus", axis=0, tiled=True)
    grad_rows = all_adjoint.shape[0] // lax.axis_size("line")
    inputs = all_adjoint
    pushed = lax.psum_scatter(
        jnp.dot(inputs, ptdf, preferred_element_type=jnp.float32),
        "line",
        scatter_dimension=0,
        tiled=True,
    )
    own_generation = lax.dynamic_slice_in_dim(
        generation, lax.axis_index("line") * grad_rows, grad_rows, 0
    ).astype(jnp.float32)
    gradient = (cost_quad[None, :] * own_generation + pushed).astype(jnp.bfloat16)
    return (gradient, outflow, outage_sens)


def solution(mesh):
    placed = (
        P(None, "bus"),
        P(None, "bus"),
        P(),
        P("line", "bus"),
        P("line", None),
        P("line"),
        P("line"),
        P(),
        P("bus"),
    )
    return jax.shard_map(
        on_device,
        mesh=mesh,
        in_specs=placed,
        out_specs=(P("line", "bus"), P("bus", None), P("bus", None)),
        check_vma=False,
    )
```

profile of v0, /device:TPU:24, one launch (start us, length us, event | category | flops | bytes accessed | tf_op | source)
XLA Modules:
  0.0 545.5 jit_solution(11208969200925676231)
XLA Ops:
  7.2 3.7 subtract_convert_fusion
  11.0 4.4 fusion.9
  15.4 98.6 %reduce-scatter.3.cloned.1.call-done = f32[64,1024]{1,0:T(8,128)} async-done(((f32[1024,1024]{1,0:T(8,128)}), f32[64,1024]{1,0:T(8,128)}) %reduce-scatter.3.cloned.1.call-update) | async-done | bytes 262160 | tf_op jit(solution)/shard_map/reduce_scatter | solution.py:39
  114.2 1.1 copy.40
  115.4 1.1 gather_fusion
  116.7 37.6 %all-gather.3.cloned.1.call-done = f32[64,16384]{1,0:T(8,128)} async-done(((f32[64,1024]{1,0:T(8,128)}), f32[64,16384]{1,0:T(8,128)}) %all-gather.3.cloned.1.call-update) | async-done | bytes 4194320 | tf_op jit(solution)/shard_map/all_gather | solution.py:46
  154.3 6.9 %copy.42 = f32[64,16384]{0,1:T(8,128)} copy(f32[64,16384]{1,0:T(8,128)} %all-gather.3.cloned.1.call-done) | data formatting | bytes 8388608 | tf_op jit(solution)/shard_map/all_gather | solution.py:46
  161.2 4.4 gather_fusion.1
  165.8 108.0 %while.12 = (s32[]{:T(128)}, f32[16,4,384]{2,1,0:T(4,128)S(1)}, f32[16,4,512]{2,1,0:T(4,128)S(1)}, f32[16,4,384]{2,1,0:T(4,128)S(1)}, f32[384,512]{1,0:T(8,128)}...) while((s32[]{:T(128)}, f32[16,4,384]{2,1,0:T(4,128)S(1)}, f32[16,4,512]{2,1,0:T(4,128)S(1)}, ...), condition=%wide.region_3.4_spmd, body=%wide.region_1.0_spmd.sunk | while | flops 24377344 | bytes 2462821 | solution.py:53
  165.9 3.3 multiply_reduce_fusion.2
  169.2 3.3 fusion.17
  172.6 3.3 multiply_reduce_fusion.2
  176.0 3.3 fusion.17
  179.4 3.3 multiply_reduce_fusion.2
  182.7 3.3 fusion.17
  186.1 3.3 multiply_reduce_fusion.2
  189.5 3.3 fusion.17
  192.9 3.3 multiply_reduce_fusion.2
  196.2 3.3 fusion.17
  199.6 3.3 multiply_reduce_fusion.2
  202.9 3.3 fusion.17
  206.4 3.3 multiply_reduce_fusion.2
  209.7 3.3 fusion.17
  213.1 3.3 multiply_reduce_fusion.2
  216.4 3.3 fusion.17
  219.9 3.3 multiply_reduce_fusion.2
  223.2 3.3 fusion.17
  226.6 3.3 multiply_reduce_fusion.2
  229.9 3.3 fusion.17
  233.4 3.3 multiply_reduce_fusion.2
  236.7 3.3 fusion.17
  240.1 3.3 multiply_reduce_fusion.2
  243.4 3.3 fusion.17
  246.9 3.3 multiply_reduce_fusion.2
  250.2 3.3 fusion.17
  253.6 3.3 multiply_reduce_fusion.2
  256.9 3.3 fusion.17
  260.4 3.3 multiply_reduce_fusion.2
  263.7 3.3 fusion.17
  267.1 3.3 multiply_reduce_fusion.2
  270.4 3.3 fusion.17
  274.8 122.1 %all-reduce.2.cloned.1.call-done = f32[64,512]{1,0:T(8,128)} async-done(((f32[64,512]{1,0:T(8,128)}), f32[64,512]{1,0:T(8,128)}) %all-reduce.2.cloned.1.call-update) | async-done | bytes 131088 | tf_op jit(solution)/shard_map/psum | solution.py:58
  396.9 1.9 fusion.1
  398.8 2.8 scatter_custom_fusion
  402.5 60.2 %all-gather.5.cloned.1.call-done = bf16[1024,1024]{1,0:T(8,128)(2,1)} async-done(((bf16[64,1024]{1,0:T(8,128)(2,1)}), bf16[1024,1024]{1,0:T(8,128)(2,1)}) %all-gather.5.cloned.1.call-update) | async-done | bytes 2097168 | tf_op jit(solution)/shard_map/all_gather | solution.py:64
  462.7 5.9 %fusion.10 = f32[1024,1024]{1,0:T(8,128)} fusion(bf16[1024,1024]{1,0:T(8,128)(2,1)} %all-gather.5.cloned.1.call-done, bf16[1024,1024]{1,0:T(8,128)(2,1)S(1)} %copy-done), kind=kOutput, calls=%fused_computation.34 | convolution fusion | flops 2147483648 | bytes 8388608 | tf_op jit(solution)/shard_map/dot_general | solution.py:68
  470.2 67.1 %reduce-scatter.5.cloned.1.call-done = f32[64,1024]{1,0:T(8,128)} async-done(((f32[1024,1024]{1,0:T(8,128)}), f32[64,1024]{1,0:T(8,128)}) %reduce-scatter.5.cloned.1.call-update) | async-done | bytes 262160 | tf_op jit(solution)/shard_map/reduce_scatter | solution.py:67
  537.3 1.7 add_convert_fusion
  (106 shorter events, 4.6 us)
Async XLA Ops:
  7.2 3.8 copy-start
  7.2 106.8 %reduce-scatter.3.cloned.1.call-start = ((), (), s32[]{:S(2)}) async-start(), calls=%async_computation.2 | async-start | bytes 4456448 | tf_op jit(solution)/shard_map/reduce_scatter | solution.py:39
  15.3 98.8 %copy-start.4 = (s32[384]{0:T(512)S(1)}, s32[384]{0:T(512)}, u32[]{:S(2)}) copy-start(s32[384]{0:T(512)} %param.17) | copy-start | bytes 4612
  15.3 98.8 %copy-start.2 = (s32[512]{0:T(512)S(1)}, s32[512]{0:T(512)}, u32[]{:S(2)}) copy-start(s32[512]{0:T(512)} %param.18) | copy-start | bytes 6148
  15.4 138.9 %all-gather.3.cloned.1.call-start = ((), (), s32[]{:S(2)}) async-start(), calls=%async_computation.3 | async-start | bytes 4456448 | tf_op jit(solution)/shard_map/all_gather | solution.py:46
  114.0 282.9 %all-reduce.2.cloned.1.call-start = ((), (), s32[]{:S(2)}) async-start(), calls=%async_computation.4 | async-start | bytes 262144 | tf_op jit(solution)/shard_map/psum | solution.py:58
  116.7 49.1 %copy-start.5 = (f32[384]{0:T(512)S(1)}, f32[384]{0:T(512)}, u32[]{:S(2)}) copy-start(f32[384]{0:T(512)} %param.16) | copy-start | bytes 4612
  274.5 188.2 %all-gather.5.cloned.1.call-start = ((), (), s32[]{:S(2)}) async-start(), calls=%async_computation.5 | async-start | bytes 2228224 | tf_op jit(solution)/shard_map/all_gather | solution.py:64
  402.5 134.8 %reduce-scatter.5.cloned.1.call-start = ((), (), s32[]{:S(2)}) async-start(), calls=%async_computation.6 | async-start | bytes 4456448 | tf_op jit(solution)/shard_map/reduce_scatter | solution.py:67
  468.6 1.0 copy-start.1
  468.6 68.7 %copy-start.3 = (f32[1024]{0:T(1024)S(1)}, f32[1024]{0:T(1024)}, u32[]{:S(2)}) copy-start(f32[1024]{0:T(1024)} %param.19) | copy-start | bytes 12292
Sparse Core Ops, SparseCore 0:
  15.5 98.4 reduce-scatter.2
  115.8 38.4 all-gather.2
  274.7 122.1 all-reduce.1
  402.6 60.0 all-gather.4
  468.7 68.4 reduce-scatter.4
where the time goes:
time: 547 us; the launch traced here: 545 us
  waiting for transfers between devices  386 us (71%)
  other arithmetic  112 us (20%)
  local copies, waits for them, and re-layouts  16.8 us (3%)
  matrix products  15.9 us (3%)
  between operations  14 us (3%)
    psum x1, waiting for transfers between devices, on_device(): sens_total = lax.psum(sens_part, 'line')  122 us
    reduce_scatter x1, waiting for transfers between devices, on_device(): lax.psum_scatter(lax.dot_general(inputs, ptdf, (((1,), (1,)), ((), ())),...  98.6 us
    reduce_scatter x1, waiting for transfers between devices, on_device(): lax.psum_scatter(jnp.dot(inputs, ptdf, preferred_element_type=jnp.float32...  67.1 us
    all_gather x1, waiting for transfers between devices, on_device(): all_adjoint = lax.all_gather(adjoint_half, 'bus', axis=0, tiled=True)  60.2 us
    reduce_sum x16, other arithmetic, contingency(): direct = jnp.sum(raw_slope, axis=2) / outage_total  53.5 us
    dot_general x16, other arithmetic, contingency(): jnp.einsum('smk,mk->sk', raw_slope, lodf, precision=lax.Precision.HIGHEST)  53.1 us
    all_gather x1, waiting for transfers between devices, on_device(): entire_flows = lax.all_gather(flow_field, 'line', axis=1, tiled=True)  37.6 us
  transfers between devices with their start and end apart: 5, of which 5 were waited for; matrix products, arithmetic and copies ran while one was open for 1% of the time, Pallas kernels for 0%

commit v1 on v0

--- a/solution.py
+++ b/solution.py
@@ -55,7 +55,7 @@
     )
     direct = direct.reshape(scen_rows, monitor_count)
     sens_part = sens_part.reshape(scen_rows, outage_total)
-    sens_total = lax.psum(sens_part, "line")
+    sens_total = jnp.sum(lax.all_gather(sens_part, "line"), axis=0)
     backward = sens_total / outage_total
     outage_sens = sens_total / math.sqrt(monitored_total)
     adjoint = jnp.zeros((scen_rows, line_rows), jnp.float32).at[:, local_monitored].add(direct)

time: 547 us -> 460 us (0.84)
  waiting for transfers between devices: 386 us -> 298 us
    psum x1 -> x0, waiting for transfers between devices: 122 us -> none  [on_device(): sens_total = lax.psum(sens_part, 'line')]
    all_gather x0 -> x1, waiting for transfers between devices: none -> 36.4 us  [on_device(): sens_total = jnp.sum(lax.all_gather(sens_part, 'line'), axis=0)]
where the time goes in v1:
time: 460 us; the launch traced here: 459 us
  waiting for transfers between devices  298 us (65%)
  other arithmetic  114 us (25%)
  local copies, waits for them, and re-layouts  16.8 us (4%)
  matrix products  14.9 us (3%)
  between operations  14 us (3%)
    reduce_scatter x1, waiting for transfers between devices, on_device(): lax.psum_scatter(lax.dot_general(inputs, ptdf, (((1,), (1,)), ((), ())),...  98.6 us
    reduce_scatter x1, waiting for transfers between devices, on_device(): lax.psum_scatter(jnp.dot(inputs, ptdf, preferred_element_type=jnp.float32...  67.1 us
    all_gather x1, waiting for transfers between devices, on_device(): all_adjoint = lax.all_gather(adjoint_half, 'bus', axis=0, tiled=True)  58.6 us
    reduce_sum x16, other arithmetic, contingency(): direct = jnp.sum(raw_slope, axis=2) / outage_total  53.5 us
    dot_general x16, other arithmetic, contingency(): jnp.einsum('smk,mk->sk', raw_slope, lodf, precision=lax.Precision.HIGHEST)  53.1 us
    all_gather x1, waiting for transfers between devices, on_device(): entire_flows = lax.all_gather(flow_field, 'line', axis=1, tiled=True)  37.6 us
    all_gather x1, waiting for transfers between devices, on_device(): sens_total = jnp.sum(lax.all_gather(sens_part, 'line'), axis=0)  36.4 us
  transfers between devices with their start and end apart: 5, of which 5 were waited for; matrix products, arithmetic and copies ran while one was open for 1% of the time, Pallas kernels for 0%

profile of v1, /device:TPU:24, one launch (start us, length us, event | category | flops | bytes accessed | tf_op | source)
XLA Modules:
  0.0 459.0 jit_solution(13945753802286077164)
XLA Ops:
  7.2 3.7 subtract_convert_fusion
  11.0 4.4 fusion.9
  15.4 98.6 %reduce-scatter.3.cloned.1.call-done = f32[64,1024]{1,0:T(8,128)} async-done(((f32[1024,1024]{1,0:T(8,128)}), f32[64,1024]{1,0:T(8,128)}) %reduce-scatter.3.cloned.1.call-update) | async-done | bytes 262160 | tf_op jit(solution)/shard_map/reduce_scatter | solution.py:39
  114.2 1.1 copy.40
  115.3 1.1 gather_fusion
  116.7 37.6 %all-gather.4.cloned.1.call-done = f32[64,16384]{1,0:T(8,128)} async-done(((f32[64,1024]{1,0:T(8,128)}), f32[64,16384]{1,0:T(8,128)}) %all-gather.4.cloned.1.call-update) | async-done | bytes 4194320 | tf_op jit(solution)/shard_map/all_gather | solution.py:46
  154.3 6.9 %copy.42 = f32[64,16384]{0,1:T(8,128)} copy(f32[64,16384]{1,0:T(8,128)} %all-gather.4.cloned.1.call-done) | data formatting | bytes 8388608 | tf_op jit(solution)/shard_map/all_gather | solution.py:46
  161.2 4.4 gather_fusion.1
  165.8 108.0 %while.12 = (s32[]{:T(128)}, f32[16,4,384]{2,1,0:T(4,128)S(1)}, f32[16,4,512]{2,1,0:T(4,128)S(1)}, f32[16,4,384]{2,1,0:T(4,128)S(1)}, f32[384,512]{1,0:T(8,128)}...) while((s32[]{:T(128)}, f32[16,4,384]{2,1,0:T(4,128)S(1)}, f32[16,4,512]{2,1,0:T(4,128)S(1)}, ...), condition=%wide.region_3.4_spmd, body=%wide.region_1.0_spmd.sunk | while | flops 24377344 | bytes 2462821 | solution.py:53
  165.9 3.3 multiply_reduce_fusion.2
  169.2 3.3 fusion.17
  172.6 3.3 multiply_reduce_fusion.2
  175.9 3.3 fusion.17
  179.4 3.3 multiply_reduce_fusion.2
  182.7 3.3 fusion.17
  186.1 3.3 multiply_reduce_fusion.2
  189.4 3.3 fusion.17
  192.9 3.3 multiply_reduce_fusion.2
  196.2 3.3 fusion.17
  199.6 3.3 multiply_reduce_fusion.2
  202.9 3.3 fusion.17
  206.4 3.3 multiply_reduce_fusion.2
  209.7 3.3 fusion.17
  213.1 3.3 multiply_reduce_fusion.2
  216.4 3.3 fusion.17
  219.9 3.3 multiply_reduce_fusion.2
  223.2 3.3 fusion.17
  226.6 3.3 multiply_reduce_fusion.2
  229.9 3.3 fusion.17
  233.3 3.3 multiply_reduce_fusion.2
  236.7 3.3 fusion.17
  240.1 3.3 multiply_reduce_fusion.2
  243.4 3.3 fusion.17
  246.8 3.3 multiply_reduce_fusion.2
  250.2 3.3 fusion.17
  253.6 3.3 multiply_reduce_fusion.2
  256.9 3.3 fusion.17
  260.3 3.3 multiply_reduce_fusion.2
  263.7 3.3 fusion.17
  267.1 3.3 multiply_reduce_fusion.2
  270.4 3.3 fusion.17
  274.7 36.4 %all-gather.6.cloned.1.call-done = f32[16,64,512]{2,1,0:T(8,128)} async-done(((f32[1,64,512]{2,1,0:T(8,128)}), f32[16,64,512]{2,1,0:T(8,128)}) %all-gather.6.cloned.1.call-update) | async-done | bytes 2097168 | tf_op jit(solution)/shard_map/all_gather | solution.py:58
  311.2 1.8 reduce_sum.18
  313.9 2.8 scatter_custom_fusion
  317.6 58.6 %all-gather.8.cloned.1.call-done = bf16[1024,1024]{1,0:T(8,128)(2,1)} async-done(((bf16[64,1024]{1,0:T(8,128)(2,1)}), bf16[1024,1024]{1,0:T(8,128)(2,1)}) %all-gather.8.cloned.1.call-update) | async-done | bytes 2097168 | tf_op jit(solution)/shard_map/all_gather | solution.py:64
  376.3 5.9 %fusion.10 = f32[1024,1024]{1,0:T(8,128)} fusion(bf16[1024,1024]{1,0:T(8,128)(2,1)} %all-gather.8.cloned.1.call-done, bf16[1024,1024]{1,0:T(8,128)(2,1)S(1)} %copy-done), kind=kOutput, calls=%fused_computation.34 | convolution fusion | flops 2147483648 | bytes 8388608 | tf_op jit(solution)/shard_map/dot_general | solution.py:68
  383.8 67.1 %reduce-scatter.5.cloned.1.call-done = f32[64,1024]{1,0:T(8,128)} async-done(((f32[1024,1024]{1,0:T(8,128)}), f32[64,1024]{1,0:T(8,128)}) %reduce-scatter.5.cloned.1.call-update) | async-done | bytes 262160 | tf_op jit(solution)/shard_map/reduce_scatter | solution.py:67
  450.8 1.7 add_convert_fusion
  (105 shorter events, 5.6 us)
Async XLA Ops:
  7.2 3.8 copy-start
  7.2 106.8 %reduce-scatter.3.cloned.1.call-start = ((), (), s32[]{:S(2)}) async-start(), calls=%async_computation.2 | async-start | bytes 4456448 | tf_op jit(solution)/shard_map/reduce_scatter | solution.py:39
  15.3 98.8 %copy-start.3 = (s32[384]{0:T(512)S(1)}, s32[384]{0:T(512)}, u32[]{:S(2)}) copy-start(s32[384]{0:T(512)} %param.17) | copy-start | bytes 4612
  15.3 98.8 %copy-start.1 = (s32[512]{0:T(512)S(1)}, s32[512]{0:T(512)}, u32[]{:S(2)}) copy-start(s32[512]{0:T(512)} %param.18) | copy-start | bytes 6148
  15.4 138.9 %all-gather.4.cloned.1.call-start = ((), (), s32[]{:S(2)}) async-start(), calls=%async_computation.3 | async-start | bytes 4456448 | tf_op jit(solution)/shard_map/all_gather | solution.py:46
  114.0 197.1 %all-gather.6.cloned.1.call-start = ((), (), s32[]{:S(2)}) async-start(), calls=%async_computation.4 | async-start | bytes 2228224 | tf_op jit(solution)/shard_map/all_gather | solution.py:58
  116.7 49.2 %copy-start.4 = (f32[384]{0:T(512)S(1)}, f32[384]{0:T(512)}, u32[]{:S(2)}) copy-start(f32[384]{0:T(512)} %param.16) | copy-start | bytes 4612
  274.5 101.8 %all-gather.8.cloned.1.call-start = ((), (), s32[]{:S(2)}) async-start(), calls=%async_computation.5 | async-start | bytes 2228224 | tf_op jit(solution)/shard_map/all_gather | solution.py:64
  317.6 133.2 %reduce-scatter.5.cloned.1.call-start = ((), (), s32[]{:S(2)}) async-start(), calls=%async_computation.6 | async-start | bytes 4456448 | tf_op jit(solution)/shard_map/reduce_scatter | solution.py:67
  382.1 68.7 %copy-start.2 = (f32[1024]{0:T(1024)S(1)}, f32[1024]{0:T(1024)}, u32[]{:S(2)}) copy-start(f32[1024]{0:T(1024)} %param.19) | copy-start | bytes 12292
Sparse Core Ops, SparseCore 0:
  15.5 98.4 reduce-scatter.2
  115.8 38.4 all-gather.3
  274.6 36.4 all-gather.5
  317.7 58.5 all-gather.7
  382.3 68.4 reduce-scatter.4
